TPU v7x, 32 devices: a whole 2x2x4 slice. The times are simulated.
32 devices in a mesh: test: 4 (over z), cell: 8 (over y, x, core).
Axes of the slice: x: 2, y: 2, z: 4, core: 2. Of those that a mesh axis runs over, the one named last changes fastest.
Arguments:
- log_perm: float32 [128, 16, 256], P('cell'), may hold values from -1 to 1
- panel: float32 [8, 128, 16, 256], P('test', 'cell'), may hold values from -4 to 4
- wells: int32 [4, 8], P('test'), may hold values from 0 to 524287
- rates: float32 [4, 8], P('test'), may hold values from 1 to 10
- recharge: float32 [4, 128, 16, 256], P('test', 'cell'), may hold values from 0.25 to 4
- gauge: float32 [128, 16, 256], P('cell'), may hold values from 0.25 to 4
Outputs:
- hessian_panel: float32 [8, 128, 16, 256], P('test', 'cell')
Inputs may be any that keep to these rules, and one draw needn't show every extreme that they name: `wells`: each entry names a cell of the whole grid, numbered x * 16 * 256 + y * 256 + z; a test may name a cell more than once.
All inputs are finite; a program needn't handle non-finite values.
Results may differ from a plain program's by a relative error of at most 0.0001.
Values sent between devices are 32-bit elements; how exact they have to be, the bound alone decides.
No kernel may reach another device: no remote copies, remote signals or barrier semaphores. Data moves between devices by JAX's collectives and lax.ppermute only.
A program may use at most 64 MiB of HBM per device.

v0:
```python
import math
import jax
import jax.numpy as jnp
import numpy as np
from jax import lax
from jax.sharding import PartitionSpec as P

CHEB = 4
storage = 0.02


def with_halo(cells, sides, width):
    for axis, dim in sides:
        count = lax.axis_size(axis)
        ends = count - 1
        head = lax.slice_in_dim(cells, 0, width, axis=dim)
        tail = lax.slice_in_dim(cells, cells.shape[dim] - width, cells.shape[dim], axis=dim)
        cells = jnp.concatenate(
            [
                lax.ppermute(tail, axis, [(i, (i + 1) % count) for i in range(ends)]),
                cells,
                lax.ppermute(head, axis, [((i + 1) % count, i) for i in range(ends)]),
            ],
            axis=dim,
        )
    return cells


def cheb_table(count):
    highest = storage + 12.0 * math.e
    theta = 0.5 * (highest + storage)
    spread = 0.5 * (highest - storage)
    sigma = theta / spread
    rho = 1.0 / sigma
    keeps = []
    pushes = []
    for turn in range(count):
        after = 1.0 / (2.0 * sigma - rho)
        keeps.append(after * rho)
        pushes.append(2.0 * after / spread)
        rho = after
    return (1.0 / theta, keeps, pushes)


def neighbours(field, back):
    axis = field.ndim - back
    widths = [(0, 0)] * field.ndim
    widths[axis] = (1, 1)
    padded = jnp.pad(field, widths)
    length = field.shape[axis]
    return (
        lax.slice_in_dim(padded, 2, length + 2, axis=axis),
        lax.slice_in_dim(padded, 0, length, axis=axis),
    )


def diffuse(weight_ext, field_ext):
    weight = weight_ext[..., 1:-1, :, :]
    field = field_ext[..., 1:-1, :, :]
    total = 0.5 * (weight + weight_ext[..., 2:, :, :]) * (field - field_ext[..., 2:, :, :])
    total = total + 0.5 * (weight + weight_ext[..., :-2, :, :]) * (
        field - field_ext[..., :-2, :, :]
    )
    for back in (2, 1):
        weight_up, weight_down = neighbours(weight, back)
        field_up, field_down = neighbours(field, back)
        total = (
            total
            + 0.5 * (weight + weight_up) * (field - field_up)
            + 0.5 * (weight + weight_down) * (field - field_down)
        )
    return total


def pairs(left_ext, right_ext):
    left = left_ext[..., 1:-1, :, :]
    right = right_ext[..., 1:-1, :, :]
    total = (left - left_ext[..., 2:, :, :]) * (right - right_ext[..., 2:, :, :])
    total = total + (left - left_ext[..., :-2, :, :]) * (right - right_ext[..., :-2, :, :])
    for back in (2, 1):
        left_up, left_down = neighbours(left, back)
        right_up, right_down = neighbours(right, back)
        total = (
            total
            + (left - left_up) * (right - right_up)
            + (left - left_down) * (right - right_down)
        )
    return total


def rims(field):
    return with_halo(field, (("cell", 1),), 1)


def shards(log_perm, panel, wells, rates, recharge, gauge):
    place = lax.axis_index("cell")
    slab, rows_y, depth_z = log_perm.shape
    tests_here, well_count = wells.shape
    first, keeps, pushes = cheb_table(CHEB)
    keep_table = jnp.asarray(np.array(keeps, np.float32))
    push_table = jnp.asarray(np.array(pushes, np.float32))
    columns = lax.all_gather(panel, "test", axis=0, tiled=True)
    columns_all = columns.shape[0]
    perm = jnp.exp(log_perm)
    stacked = jnp.concatenate([perm[None], perm[None] * columns], axis=0)
    coeff_ext = with_halo(stacked, (("cell", 1),), 2)
    perm_ext = coeff_ext[0]
    scaled_ext = coeff_ext[1:, 1:-1]
    cells = slab * rows_y * depth_z
    flat = place * cells + jnp.arange(cells, dtype=jnp.int32)
    hits = wells[:, :, None] == flat[None, None, :]
    points = jnp.sum(jnp.where(hits, rates[:, :, None], 0.0), axis=1).reshape(
        tests_here, slab, rows_y, depth_z
    )
    counts = jnp.sum(hits.astype(jnp.float32), axis=1).reshape(tests_here, slab, rows_y, depth_z)
    source = recharge + points
    observe = gauge[None] + counts

    def solve(right_side):
        solution = jnp.zeros_like(right_side)
        residual = right_side
        direction = right_side * first

        def sweep(turn, carry):
            solution, residual, direction = carry
            extended = with_halo(direction, (("cell", 1),), 1)
            image = storage * direction + diffuse(perm_ext[1:-1], extended)
            solution = solution + direction
            residual = residual - image
            direction = keep_table[turn] * direction + push_table[turn] * residual
            return (solution, residual, direction)

        solution, residual, direction = lax.fori_loop(
            0, CHEB, sweep, (solution, residual, direction)
        )
        return solution + direction

    state = solve(source)
    state_ext = rims(state)
    forcing = -diffuse(scaled_ext, state_ext[:, None])
    forcing = forcing.reshape(tests_here * columns_all, slab, rows_y, depth_z)
    change = solve(forcing)
    weighted = (
        change.reshape(tests_here, columns_all, slab, rows_y, depth_z) * observe[:, None]
    ).reshape(tests_here * columns_all, slab, rows_y, depth_z)
    adjoint = solve(weighted)
    adjoint_ext = rims(adjoint).reshape(tests_here, columns_all, slab + 2, rows_y, depth_z)
    contrib = jnp.sum(pairs(state_ext[:, None], adjoint_ext), axis=0)
    partial_value = -0.5 * perm[None] * contrib
    total = lax.psum(partial_value, "test")
    share = panel.shape[0]
    owned = lax.dynamic_slice_in_dim(total, lax.axis_index("test") * share, share, 0)
    return owned


def solution(mesh):
    return jax.shard_map(
        shards,
        mesh=mesh,
        in_specs=(
            P("cell", None, None),
            P("test", "cell", None, None),
            P("test", None),
            P("test", None),
            P("test", "cell", None, None),
            P("cell", None, None),
        ),
        out_specs=P("test", "cell", None, None),
        check_vma=False,
    )
```

profile of v0, /device:TPU:0, one launch (start us, length us, event | category | flops | bytes accessed | tf_op | source)
XLA Modules:
  0.0 408.5 jit_solution(683576134354521020)
XLA Ops:
  9.1 48.2 %all-gather.2.cloned.1.call-done = f32[8,16,16,256]{3,2,1,0:T(8,128)} async-done(((f32[2,16,16,256]{3,2,1,0:T(8,128)}), f32[8,16,16,256]{3,2,1,0:T(8,128)}) %all-gather.2.cloned.1.call-update) | async-done | bytes 2097168 | tf_op jit(solution)/shard_map/all_gather | solution.py:102
  70.8 51.1 %while.63 = (s32[]{:T(128)}, f32[1,16,16,256]{3,2,1,0:T(8,128)}, f32[1,16,16,256]{3,2,1,0:T(8,128)}, f32[1,16,16,256]{3,2,1,0:T(8,128)}, f32[16,16,256]{2,1,0:T(...) while((s32[]{:T(128)}, f32[1,16,16,256]{3,2,1,0:T(8,128)}, ...), condition=%wide.region_2.3_spmd.clone.clone, body=%wide.region_1.2_spmd.sunk.clone.clone.sunk | while | flops 2424835 | bytes 3637479 | solution.py:133
  80.0 3.5 multiply_add_fusion.6
  84.4 4.4 %collective-permute-start = (f32[1,1,16,256]{3,2,1,0:T(8,128)S(1)}, f32[1,1,16,256]{3,2,1,0:T(8,128)S(1)}, u32[]{:S(2)}, u32[]{:S(2)}) collective-permute-start(f32[1,1,16,256]{3,2,1,0:T(8,128)S(1)} %get-tuple-element.979), channel_id=1, source_target_pairs={{0,1},{1,2},{2,3},{3,4},{4,5},{5,6},{6,7},{8,9},{9,10},{10,11},{11... | collective-permute-start | bytes 49160 | tf_op jit(solution)/shard_map/while/body/eval_jaxpr/ppermute | solution.py:20
  92.1 3.6 multiply_add_fusion.6
  96.7 6.0 %collective-permute-start = (f32[1,1,16,256]{3,2,1,0:T(8,128)S(1)}, f32[1,1,16,256]{3,2,1,0:T(8,128)S(1)}, u32[]{:S(2)}, u32[]{:S(2)}) collective-permute-start(f32[1,1,16,256]{3,2,1,0:T(8,128)S(1)} %get-tuple-element.979), channel_id=1, source_target_pairs={{0,1},{1,2},{2,3},{3,4},{4,5},{5,6},{6,7},{8,9},{9,10},{10,11},{11... | collective-permute-start | bytes 49160 | tf_op jit(solution)/shard_map/while/body/eval_jaxpr/ppermute | solution.py:20
  105.8 3.6 multiply_add_fusion.6
  110.3 4.8 %collective-permute-start = (f32[1,1,16,256]{3,2,1,0:T(8,128)S(1)}, f32[1,1,16,256]{3,2,1,0:T(8,128)S(1)}, u32[]{:S(2)}, u32[]{:S(2)}) collective-permute-start(f32[1,1,16,256]{3,2,1,0:T(8,128)S(1)} %get-tuple-element.979), channel_id=1, source_target_pairs={{0,1},{1,2},{2,3},{3,4},{4,5},{5,6},{6,7},{8,9},{9,10},{10,11},{11... | collective-permute-start | bytes 49160 | tf_op jit(solution)/shard_map/while/body/eval_jaxpr/ppermute | solution.py:20
  118.2 3.6 multiply_add_fusion.6
  122.9 4.8 %collective-permute-start.8 = (f32[1,1,16,256]{3,2,1,0:T(8,128)S(1)}, f32[1,1,16,256]{3,2,1,0:T(8,128)S(1)}, u32[]{:S(2)}, u32[]{:S(2)}) collective-permute-start(f32[1,1,16,256]{3,2,1,0:T(8,128)S(1)} %get-tuple-element.831), channel_id=1, source_target_pairs={{0,1},{1,2},{2,3},{3,4},{4,5},{5,6},{6,7},{8,9},{9,10},{10,11},{11... | collective-permute-start | bytes 49160 | tf_op jit(solution)/shard_map/ppermute | solution.py:20
  133.3 4.0 broadcast_multiply_fusion.5
  137.3 76.5 %while.64 = (s32[]{:T(128)}, f32[8,16,16,256]{3,2,1,0:T(8,128)}, f32[8,16,16,256]{3,2,1,0:T(8,128)}, f32[8,16,16,256]{3,2,1,0:T(8,128)}, f32[16,16,256]{2,1,0:T(...) while((s32[]{:T(128)}, f32[8,16,16,256]{3,2,1,0:T(8,128)}, ...), condition=%wide.region_4.5_spmd.clone.clone, body=%wide.region_3.4_spmd.sunk.clone.clone.sunk | while | flops 14811139 | bytes 23068904 | solution.py:133
  139.6 4.5 %collective-permute-start.2 = (f32[8,1,16,256]{3,2,1,0:T(8,128)}, f32[8,1,16,256]{3,2,1,0:T(8,128)}, u32[]{:S(2)}, u32[]{:S(2)}) collective-permute-start(f32[8,1,16,256]{3,2,1,0:T(8,128)} %get-tuple-element.995), channel_id=1, source_target_pairs={{0,1},{1,2},{2,3},{3,4},{4,5},{5,6},{6,7},{8,9},{9,10},{10,11},{11... | collective-permute-start | bytes 393224 | tf_op jit(solution)/shard_map/while/body/eval_jaxpr/ppermute | solution.py:20
  147.8 7.1 %multiply_add_fusion.7 = (f32[8,16,16,256]{3,2,1,0:T(8,128)}, f32[8,16,16,256]{3,2,1,0:T(8,128)}, f32[8,16,16,256]{3,2,1,0:T(8,128)}) fusion(f32[8,16,16,256]{3,2,1,0:T(8,128)S(1)} %copy.50, f32[]{:T(128)} %bitcast.98, f32[]{:T(128)} %bitcast.99, f32[8,16,16,256]{3,2,1,0:T(8,128)} %get-tuple-element.1066, f32[16,16,256]{2,1,0:T(8,128)S(1)} %get-tuple-element.991, ...), kind=kLoop, calls=%fused_computation.69.clone.1 | loop fusion | flops 14155776 | bytes 14417929 | tf_op jit(solution)/shard_map/while/body/eval_jaxpr/add | solution.py:130
  157.3 6.1 %collective-permute-start.2 = (f32[8,1,16,256]{3,2,1,0:T(8,128)}, f32[8,1,16,256]{3,2,1,0:T(8,128)}, u32[]{:S(2)}, u32[]{:S(2)}) collective-permute-start(f32[8,1,16,256]{3,2,1,0:T(8,128)} %get-tuple-element.995), channel_id=1, source_target_pairs={{0,1},{1,2},{2,3},{3,4},{4,5},{5,6},{6,7},{8,9},{9,10},{10,11},{11... | collective-permute-start | bytes 393224 | tf_op jit(solution)/shard_map/while/body/eval_jaxpr/ppermute | solution.py:20
  167.0 7.5 %multiply_add_fusion.7 = (f32[8,16,16,256]{3,2,1,0:T(8,128)}, f32[8,16,16,256]{3,2,1,0:T(8,128)}, f32[8,16,16,256]{3,2,1,0:T(8,128)}) fusion(f32[8,16,16,256]{3,2,1,0:T(8,128)S(1)} %copy.50, f32[]{:T(128)} %bitcast.98, f32[]{:T(128)} %bitcast.99, f32[8,16,16,256]{3,2,1,0:T(8,128)} %get-tuple-element.1066, f32[16,16,256]{2,1,0:T(8,128)S(1)} %get-tuple-element.991, ...), kind=kLoop, calls=%fused_computation.69.clone.1 | loop fusion | flops 14155776 | bytes 14417929 | tf_op jit(solution)/shard_map/while/body/eval_jaxpr/add | solution.py:130
  176.7 6.7 %collective-permute-start.2 = (f32[8,1,16,256]{3,2,1,0:T(8,128)}, f32[8,1,16,256]{3,2,1,0:T(8,128)}, u32[]{:S(2)}, u32[]{:S(2)}) collective-permute-start(f32[8,1,16,256]{3,2,1,0:T(8,128)} %get-tuple-element.995), channel_id=1, source_target_pairs={{0,1},{1,2},{2,3},{3,4},{4,5},{5,6},{6,7},{8,9},{9,10},{10,11},{11... | collective-permute-start | bytes 393224 | tf_op jit(solution)/shard_map/while/body/eval_jaxpr/ppermute | solution.py:20
  187.1 7.5 %multiply_add_fusion.7 = (f32[8,16,16,256]{3,2,1,0:T(8,128)}, f32[8,16,16,256]{3,2,1,0:T(8,128)}, f32[8,16,16,256]{3,2,1,0:T(8,128)}) fusion(f32[8,16,16,256]{3,2,1,0:T(8,128)S(1)} %copy.50, f32[]{:T(128)} %bitcast.98, f32[]{:T(128)} %bitcast.99, f32[8,16,16,256]{3,2,1,0:T(8,128)} %get-tuple-element.1066, f32[16,16,256]{2,1,0:T(8,128)S(1)} %get-tuple-element.991, ...), kind=kLoop, calls=%fused_computation.69.clone.1 | loop fusion | flops 14155776 | bytes 14417929 | tf_op jit(solution)/shard_map/while/body/eval_jaxpr/add | solution.py:130
  196.8 5.8 %collective-permute-start.2 = (f32[8,1,16,256]{3,2,1,0:T(8,128)}, f32[8,1,16,256]{3,2,1,0:T(8,128)}, u32[]{:S(2)}, u32[]{:S(2)}) collective-permute-start(f32[8,1,16,256]{3,2,1,0:T(8,128)} %get-tuple-element.995), channel_id=1, source_target_pairs={{0,1},{1,2},{2,3},{3,4},{4,5},{5,6},{6,7},{8,9},{9,10},{10,11},{11... | collective-permute-start | bytes 393224 | tf_op jit(solution)/shard_map/while/body/eval_jaxpr/ppermute | solution.py:20
  206.3 7.5 %multiply_add_fusion.7 = (f32[8,16,16,256]{3,2,1,0:T(8,128)}, f32[8,16,16,256]{3,2,1,0:T(8,128)}, f32[8,16,16,256]{3,2,1,0:T(8,128)}) fusion(f32[8,16,16,256]{3,2,1,0:T(8,128)S(1)} %copy.50, f32[]{:T(128)} %bitcast.98, f32[]{:T(128)} %bitcast.99, f32[8,16,16,256]{3,2,1,0:T(8,128)} %get-tuple-element.1066, f32[16,16,256]{2,1,0:T(8,128)S(1)} %get-tuple-element.991, ...), kind=kLoop, calls=%fused_computation.69.clone.1 | loop fusion | flops 14155776 | bytes 14417929 | tf_op jit(solution)/shard_map/while/body/eval_jaxpr/add | solution.py:130
  213.7 4.9 %broadcast_multiply_fusion.4 = (f32[8,16,16,256]{3,2,1,0:T(8,128)}, f32[8,16,16,256]{3,2,1,0:T(8,128)}) fusion(f32[16,16,256]{2,1,0:T(8,128)} %add.631, f32[8,16,16,256]{3,2,1,0:T(8,128)} %get-tuple-element.571, f32[8,16,16,256]{3,2,1,0:T(8,128)} %get-tuple-element.572), kind=kLoop, calls=%fused_computation.180 | loop fusion | flops 1572864 | bytes 8650752 | tf_op jit(solution)/shard_map/mul | solution.py:122
  218.7 75.9 %while.65 = (s32[]{:T(128)}, f32[8,16,16,256]{3,2,1,0:T(8,128)}, f32[8,16,16,256]{3,2,1,0:T(8,128)}, f32[8,16,16,256]{3,2,1,0:T(8,128)}, f32[16,16,256]{2,1,0:T(...) while((s32[]{:T(128)}, f32[8,16,16,256]{3,2,1,0:T(8,128)}, ...), condition=%wide.region_7.8_spmd.clone.clone, body=%wide.region_6.7_spmd.sunk.clone.clone.sunk | while | flops 14811139 | bytes 23068904 | solution.py:133
  221.0 5.8 %collective-permute-start.4 = (f32[8,1,16,256]{3,2,1,0:T(8,128)}, f32[8,1,16,256]{3,2,1,0:T(8,128)}, u32[]{:S(2)}, u32[]{:S(2)}) collective-permute-start(f32[8,1,16,256]{3,2,1,0:T(8,128)} %get-tuple-element.1013), channel_id=1, source_target_pairs={{0,1},{1,2},{2,3},{3,4},{4,5},{5,6},{6,7},{8,9},{9,10},{10,11},{11... | collective-permute-start | bytes 393224 | tf_op jit(solution)/shard_map/while/body/eval_jaxpr/ppermute | solution.py:20
  230.3 7.0 %multiply_add_fusion.8 = (f32[8,16,16,256]{3,2,1,0:T(8,128)}, f32[8,16,16,256]{3,2,1,0:T(8,128)}, f32[8,16,16,256]{3,2,1,0:T(8,128)}) fusion(f32[8,16,16,256]{3,2,1,0:T(8,128)S(1)} %copy.51, f32[]{:T(128)} %bitcast.100, f32[]{:T(128)} %bitcast.101, f32[8,16,16,256]{3,2,1,0:T(8,128)} %get-tuple-element.1099, ...), kind=kLoop, calls=%fused_computation.110.clone.1 | loop fusion | flops 14155776 | bytes 14417929 | tf_op jit(solution)/shard_map/while/body/eval_jaxpr/add | solution.py:130
  239.6 5.8 %collective-permute-start.4 = (f32[8,1,16,256]{3,2,1,0:T(8,128)}, f32[8,1,16,256]{3,2,1,0:T(8,128)}, u32[]{:S(2)}, u32[]{:S(2)}) collective-permute-start(f32[8,1,16,256]{3,2,1,0:T(8,128)} %get-tuple-element.1013), channel_id=1, source_target_pairs={{0,1},{1,2},{2,3},{3,4},{4,5},{5,6},{6,7},{8,9},{9,10},{10,11},{11... | collective-permute-start | bytes 393224 | tf_op jit(solution)/shard_map/while/body/eval_jaxpr/ppermute | solution.py:20
  249.1 7.3 %multiply_add_fusion.8 = (f32[8,16,16,256]{3,2,1,0:T(8,128)}, f32[8,16,16,256]{3,2,1,0:T(8,128)}, f32[8,16,16,256]{3,2,1,0:T(8,128)}) fusion(f32[8,16,16,256]{3,2,1,0:T(8,128)S(1)} %copy.51, f32[]{:T(128)} %bitcast.100, f32[]{:T(128)} %bitcast.101, f32[8,16,16,256]{3,2,1,0:T(8,128)} %get-tuple-element.1099, ...), kind=kLoop, calls=%fused_computation.110.clone.1 | loop fusion | flops 14155776 | bytes 14417929 | tf_op jit(solution)/shard_map/while/body/eval_jaxpr/add | solution.py:130
  258.7 5.8 %collective-permute-start.4 = (f32[8,1,16,256]{3,2,1,0:T(8,128)}, f32[8,1,16,256]{3,2,1,0:T(8,128)}, u32[]{:S(2)}, u32[]{:S(2)}) collective-permute-start(f32[8,1,16,256]{3,2,1,0:T(8,128)} %get-tuple-element.1013), channel_id=1, source_target_pairs={{0,1},{1,2},{2,3},{3,4},{4,5},{5,6},{6,7},{8,9},{9,10},{10,11},{11... | collective-permute-start | bytes 393224 | tf_op jit(solution)/shard_map/while/body/eval_jaxpr/ppermute | solution.py:20
  268.1 7.3 %multiply_add_fusion.8 = (f32[8,16,16,256]{3,2,1,0:T(8,128)}, f32[8,16,16,256]{3,2,1,0:T(8,128)}, f32[8,16,16,256]{3,2,1,0:T(8,128)}) fusion(f32[8,16,16,256]{3,2,1,0:T(8,128)S(1)} %copy.51, f32[]{:T(128)} %bitcast.100, f32[]{:T(128)} %bitcast.101, f32[8,16,16,256]{3,2,1,0:T(8,128)} %get-tuple-element.1099, ...), kind=kLoop, calls=%fused_computation.110.clone.1 | loop fusion | flops 14155776 | bytes 14417929 | tf_op jit(solution)/shard_map/while/body/eval_jaxpr/add | solution.py:130
  277.8 5.8 %collective-permute-start.4 = (f32[8,1,16,256]{3,2,1,0:T(8,128)}, f32[8,1,16,256]{3,2,1,0:T(8,128)}, u32[]{:S(2)}, u32[]{:S(2)}) collective-permute-start(f32[8,1,16,256]{3,2,1,0:T(8,128)} %get-tuple-element.1013), channel_id=1, source_target_pairs={{0,1},{1,2},{2,3},{3,4},{4,5},{5,6},{6,7},{8,9},{9,10},{10,11},{11... | collective-permute-start | bytes 393224 | tf_op jit(solution)/shard_map/while/body/eval_jaxpr/ppermute | solution.py:20
  287.2 7.3 %multiply_add_fusion.8 = (f32[8,16,16,256]{3,2,1,0:T(8,128)}, f32[8,16,16,256]{3,2,1,0:T(8,128)}, f32[8,16,16,256]{3,2,1,0:T(8,128)}) fusion(f32[8,16,16,256]{3,2,1,0:T(8,128)S(1)} %copy.51, f32[]{:T(128)} %bitcast.100, f32[]{:T(128)} %bitcast.101, f32[8,16,16,256]{3,2,1,0:T(8,128)} %get-tuple-element.1099, ...), kind=kLoop, calls=%fused_computation.110.clone.1 | loop fusion | flops 14155776 | bytes 14417929 | tf_op jit(solution)/shard_map/while/body/eval_jaxpr/add | solution.py:130
  297.3 5.2 %collective-permute-start.10 = (f32[8,1,16,256]{3,2,1,0:T(8,128)S(1)}, f32[8,1,16,256]{3,2,1,0:T(8,128)S(1)}, u32[]{:S(2)}, u32[]{:S(2)}) collective-permute-start(f32[8,1,16,256]{3,2,1,0:T(8,128)S(1)} %get-tuple-element.818), channel_id=1, source_target_pairs={{0,1},{1,2},{2,3},{3,4},{4,5},{5,6},{6,7},{8,9},{9,10},{10,11},{11... | collective-permute-start | bytes 393224 | tf_op jit(solution)/shard_map/ppermute | solution.py:20
  310.7 89.1 %all-reduce.20.cloned.1.call-done = f32[8,16,16,256]{3,2,1,0:T(8,128)} async-done(((f32[8,16,16,256]{3,2,1,0:T(8,128)}), f32[8,16,16,256]{3,2,1,0:T(8,128)}) %all-reduce.20.cloned.1.call-update) | async-done | bytes 2097168 | tf_op jit(solution)/shard_map/psum | solution.py:150
  (186 shorter events, 103.7 us)
Async XLA Ops:
  6.5 50.8 %all-gather.2.cloned.1.call-start = ((), (), s32[]{:S(2)}) async-start(), calls=%async_computation | async-start | bytes 2621440 | tf_op jit(solution)/shard_map/all_gather | solution.py:102
  7.3 392.5 %all-reduce.20.cloned.1.call-start = ((), (), s32[]{:S(2)}) async-start(), calls=%async_computation.1 | async-start | bytes 4194304 | tf_op jit(solution)/shard_map/psum | solution.py:150
  60.2 7.9 %collective-permute-start.6 = (f32[9,2,16,256]{3,2,1,0:T(8,128)}, f32[9,2,16,256]{3,2,1,0:T(8,128)S(1)}, u32[]{:S(2)}, u32[]{:S(2)}) collective-permute-start(f32[9,2,16,256]{3,2,1,0:T(8,128)} %get-tuple-element.817), channel_id=1, source_target_pairs={{1,0},{2,1},{3,2},{4,3},{5,4},{6,5},{7,6},{9,8},{10,9},{11,10},{12... | collective-permute-start | bytes 884744 | tf_op jit(solution)/shard_map/ppermute | solution.py:22
  61.4 6.7 %collective-permute-start.7 = (f32[9,2,16,256]{3,2,1,0:T(8,128)}, f32[9,2,16,256]{3,2,1,0:T(8,128)S(1)}, u32[]{:S(2)}, u32[]{:S(2)}) collective-permute-start(f32[9,2,16,256]{3,2,1,0:T(8,128)} %get-tuple-element.816), channel_id=1, source_target_pairs={{0,1},{1,2},{2,3},{3,4},{4,5},{5,6},{6,7},{8,9},{9,10},{10,11},{11... | collective-permute-start | bytes 884744 | tf_op jit(solution)/shard_map/ppermute | solution.py:20
  71.7 5.9 %collective-permute-start = (f32[1,1,16,256]{3,2,1,0:T(8,128)S(1)}, f32[1,1,16,256]{3,2,1,0:T(8,128)S(1)}, u32[]{:S(2)}, u32[]{:S(2)}) collective-permute-start(f32[1,1,16,256]{3,2,1,0:T(8,128)S(1)} %get-tuple-element.979), channel_id=1, source_target_pairs={{0,1},{1,2},{2,3},{3,4},{4,5},{5,6},{6,7},{8,9},{9,10},{10,11},{11... | collective-permute-start | bytes 49160 | tf_op jit(solution)/shard_map/while/body/eval_jaxpr/ppermute | solution.py:20
  75.0 5.0 %collective-permute-start.1 = (f32[1,1,16,256]{3,2,1,0:T(8,128)S(1)}, f32[1,1,16,256]{3,2,1,0:T(8,128)S(1)}, u32[]{:S(2)}, u32[]{:S(2)}) collective-permute-start(f32[1,1,16,256]{3,2,1,0:T(8,128)S(1)} %get-tuple-element.980), channel_id=1, source_target_pairs={{1,0},{2,1},{3,2},{4,3},{5,4},{6,5},{7,6},{9,8},{10,9},{11,10},{12... | collective-permute-start | bytes 49160 | tf_op jit(solution)/shard_map/while/body/eval_jaxpr/ppermute | solution.py:22
  84.4 7.0 %collective-permute-start = (f32[1,1,16,256]{3,2,1,0:T(8,128)S(1)}, f32[1,1,16,256]{3,2,1,0:T(8,128)S(1)}, u32[]{:S(2)}, u32[]{:S(2)}) collective-permute-start(f32[1,1,16,256]{3,2,1,0:T(8,128)S(1)} %get-tuple-element.979), channel_id=1, source_target_pairs={{0,1},{1,2},{2,3},{3,4},{4,5},{5,6},{6,7},{8,9},{9,10},{10,11},{11... | collective-permute-start | bytes 49160 | tf_op jit(solution)/shard_map/while/body/eval_jaxpr/ppermute | solution.py:20
  88.8 3.3 collective-permute-start.1
  96.7 8.6 %collective-permute-start = (f32[1,1,16,256]{3,2,1,0:T(8,128)S(1)}, f32[1,1,16,256]{3,2,1,0:T(8,128)S(1)}, u32[]{:S(2)}, u32[]{:S(2)}) collective-permute-start(f32[1,1,16,256]{3,2,1,0:T(8,128)S(1)} %get-tuple-element.979), channel_id=1, source_target_pairs={{0,1},{1,2},{2,3},{3,4},{4,5},{5,6},{6,7},{8,9},{9,10},{10,11},{11... | collective-permute-start | bytes 49160 | tf_op jit(solution)/shard_map/while/body/eval_jaxpr/ppermute | solution.py:20
  102.7 3.1 collective-permute-start.1
  110.3 7.4 %collective-permute-start = (f32[1,1,16,256]{3,2,1,0:T(8,128)S(1)}, f32[1,1,16,256]{3,2,1,0:T(8,128)S(1)}, u32[]{:S(2)}, u32[]{:S(2)}) collective-permute-start(f32[1,1,16,256]{3,2,1,0:T(8,128)S(1)} %get-tuple-element.979), channel_id=1, source_target_pairs={{0,1},{1,2},{2,3},{3,4},{4,5},{5,6},{6,7},{8,9},{9,10},{10,11},{11... | collective-permute-start | bytes 49160 | tf_op jit(solution)/shard_map/while/body/eval_jaxpr/ppermute | solution.py:20
  115.2 3.1 collective-permute-start.1
  122.9 8.9 %collective-permute-start.8 = (f32[1,1,16,256]{3,2,1,0:T(8,128)S(1)}, f32[1,1,16,256]{3,2,1,0:T(8,128)S(1)}, u32[]{:S(2)}, u32[]{:S(2)}) collective-permute-start(f32[1,1,16,256]{3,2,1,0:T(8,128)S(1)} %get-tuple-element.831), channel_id=1, source_target_pairs={{0,1},{1,2},{2,3},{3,4},{4,5},{5,6},{6,7},{8,9},{9,10},{10,11},{11... | collective-permute-start | bytes 49160 | tf_op jit(solution)/shard_map/ppermute | solution.py:20
  127.7 4.1 collective-permute-start.9
  139.6 8.1 %collective-permute-start.2 = (f32[8,1,16,256]{3,2,1,0:T(8,128)}, f32[8,1,16,256]{3,2,1,0:T(8,128)}, u32[]{:S(2)}, u32[]{:S(2)}) collective-permute-start(f32[8,1,16,256]{3,2,1,0:T(8,128)} %get-tuple-element.995), channel_id=1, source_target_pairs={{0,1},{1,2},{2,3},{3,4},{4,5},{5,6},{6,7},{8,9},{9,10},{10,11},{11... | collective-permute-start | bytes 393224 | tf_op jit(solution)/shard_map/while/body/eval_jaxpr/ppermute | solution.py:20
  144.0 3.8 collective-permute-start.3
  157.3 9.7 %collective-permute-start.2 = (f32[8,1,16,256]{3,2,1,0:T(8,128)}, f32[8,1,16,256]{3,2,1,0:T(8,128)}, u32[]{:S(2)}, u32[]{:S(2)}) collective-permute-start(f32[8,1,16,256]{3,2,1,0:T(8,128)} %get-tuple-element.995), channel_id=1, source_target_pairs={{0,1},{1,2},{2,3},{3,4},{4,5},{5,6},{6,7},{8,9},{9,10},{10,11},{11... | collective-permute-start | bytes 393224 | tf_op jit(solution)/shard_map/while/body/eval_jaxpr/ppermute | solution.py:20
  163.3 3.6 collective-permute-start.3
  176.7 10.3 %collective-permute-start.2 = (f32[8,1,16,256]{3,2,1,0:T(8,128)}, f32[8,1,16,256]{3,2,1,0:T(8,128)}, u32[]{:S(2)}, u32[]{:S(2)}) collective-permute-start(f32[8,1,16,256]{3,2,1,0:T(8,128)} %get-tuple-element.995), channel_id=1, source_target_pairs={{0,1},{1,2},{2,3},{3,4},{4,5},{5,6},{6,7},{8,9},{9,10},{10,11},{11... | collective-permute-start | bytes 393224 | tf_op jit(solution)/shard_map/while/body/eval_jaxpr/ppermute | solution.py:20
  183.4 3.6 collective-permute-start.3
  196.8 9.4 %collective-permute-start.2 = (f32[8,1,16,256]{3,2,1,0:T(8,128)}, f32[8,1,16,256]{3,2,1,0:T(8,128)}, u32[]{:S(2)}, u32[]{:S(2)}) collective-permute-start(f32[8,1,16,256]{3,2,1,0:T(8,128)} %get-tuple-element.995), channel_id=1, source_target_pairs={{0,1},{1,2},{2,3},{3,4},{4,5},{5,6},{6,7},{8,9},{9,10},{10,11},{11... | collective-permute-start | bytes 393224 | tf_op jit(solution)/shard_map/while/body/eval_jaxpr/ppermute | solution.py:20
  202.6 3.6 collective-permute-start.3
  221.0 9.3 %collective-permute-start.4 = (f32[8,1,16,256]{3,2,1,0:T(8,128)}, f32[8,1,16,256]{3,2,1,0:T(8,128)}, u32[]{:S(2)}, u32[]{:S(2)}) collective-permute-start(f32[8,1,16,256]{3,2,1,0:T(8,128)} %get-tuple-element.1013), channel_id=1, source_target_pairs={{0,1},{1,2},{2,3},{3,4},{4,5},{5,6},{6,7},{8,9},{9,10},{10,11},{11... | collective-permute-start | bytes 393224 | tf_op jit(solution)/shard_map/while/body/eval_jaxpr/ppermute | solution.py:20
  226.8 3.6 collective-permute-start.5
  239.6 9.4 %collective-permute-start.4 = (f32[8,1,16,256]{3,2,1,0:T(8,128)}, f32[8,1,16,256]{3,2,1,0:T(8,128)}, u32[]{:S(2)}, u32[]{:S(2)}) collective-permute-start(f32[8,1,16,256]{3,2,1,0:T(8,128)} %get-tuple-element.1013), channel_id=1, source_target_pairs={{0,1},{1,2},{2,3},{3,4},{4,5},{5,6},{6,7},{8,9},{9,10},{10,11},{11... | collective-permute-start | bytes 393224 | tf_op jit(solution)/shard_map/while/body/eval_jaxpr/ppermute | solution.py:20
  245.5 3.6 collective-permute-start.5
  258.7 9.4 %collective-permute-start.4 = (f32[8,1,16,256]{3,2,1,0:T(8,128)}, f32[8,1,16,256]{3,2,1,0:T(8,128)}, u32[]{:S(2)}, u32[]{:S(2)}) collective-permute-start(f32[8,1,16,256]{3,2,1,0:T(8,128)} %get-tuple-element.1013), channel_id=1, source_target_pairs={{0,1},{1,2},{2,3},{3,4},{4,5},{5,6},{6,7},{8,9},{9,10},{10,11},{11... | collective-permute-start | bytes 393224 | tf_op jit(solution)/shard_map/while/body/eval_jaxpr/ppermute | solution.py:20
  264.6 3.6 collective-permute-start.5
  277.8 9.4 %collective-permute-start.4 = (f32[8,1,16,256]{3,2,1,0:T(8,128)}, f32[8,1,16,256]{3,2,1,0:T(8,128)}, u32[]{:S(2)}, u32[]{:S(2)}) collective-permute-start(f32[8,1,16,256]{3,2,1,0:T(8,128)} %get-tuple-element.1013), channel_id=1, source_target_pairs={{0,1},{1,2},{2,3},{3,4},{4,5},{5,6},{6,7},{8,9},{9,10},{10,11},{11... | collective-permute-start | bytes 393224 | tf_op jit(solution)/shard_map/while/body/eval_jaxpr/ppermute | solution.py:20
  283.6 3.6 collective-permute-start.5
  297.3 6.5 %collective-permute-start.10 = (f32[8,1,16,256]{3,2,1,0:T(8,128)S(1)}, f32[8,1,16,256]{3,2,1,0:T(8,128)S(1)}, u32[]{:S(2)}, u32[]{:S(2)}) collective-permute-start(f32[8,1,16,256]{3,2,1,0:T(8,128)S(1)} %get-tuple-element.818), channel_id=1, source_target_pairs={{0,1},{1,2},{2,3},{3,4},{4,5},{5,6},{6,7},{8,9},{9,10},{10,11},{11... | collective-permute-start | bytes 393224 | tf_op jit(solution)/shard_map/ppermute | solution.py:20
  302.5 3.2 collective-permute-start.11
  (17 other events, 88.7 us)
Sparse Core Ops, SparseCore 0:
  8.9 48.3 all-gather.1
  310.8 88.8 all-reduce.19
where the time goes:
time: 410 us; the launch traced here: 408 us
  waiting for transfers between devices  144 us (35%)
  other arithmetic  110 us (27%)
  starting transfers between devices  97.2 us (24%)
  local copies, waits for them, and re-layouts  42.9 us (10%)
  between operations  13.8 us (3%)
    psum x1, waiting for transfers between devices, shards(): total = lax.psum(partial_value, 'test')  89.1 us
    ppermute x15, starting transfers between devices, with_halo(): lax.ppermute(tail, axis, [(i, (i + 1) % count) for i in range(ends)])  77.9 us
    add x12, other arithmetic, sweep(): direction = keep_table[turn] * direction + push_table[turn] * residual  72.8 us
    all_gather x1, waiting for transfers between devices, shards(): columns = lax.all_gather(panel, 'test', axis=0, tiled=True)  48.2 us
    ppermute x15, starting transfers between devices, with_halo(): lax.ppermute(head, axis, [((i + 1) % count, i) for i in range(ends)])  19.3 us
    while x12, local copies, waits for them, and re-layouts  16.5 us
    dynamic_slice x24, local copies, waits for them, and re-layouts, sweep(): direction = keep_table[turn] * direction + push_table[turn] * residual  15.1 us
    mul x3, other arithmetic, solve(): direction = right_side * first  10.7 us
  transfers between devices with their start and end apart: 32, of which 8 were waited for; matrix products, arithmetic and copies ran while one was open for 8% of the time, Pallas kernels for 0%

commit v1 on v0

--- a/solution.py
+++ b/solution.py
@@ -7,6 +7,28 @@
 
 CHEB = 4
 storage = 0.02
+
+
+def laid_out(blocks, dim):
+    shape = list(blocks.shape[1:])
+    shape[dim] *= blocks.shape[0]
+    return jnp.moveaxis(blocks, 0, dim).reshape(shape)
+
+
+def collect(shard, axis, dim):
+    peers = lax.axis_size(axis)
+    pairs = [(i, (i + 1) % peers) for i in range(peers)]
+    back = [(b, a) for a, b in pairs]
+    lower, upper = ([], [])
+    for turn in range(peers - 1):
+        if turn % 2 == 0:
+            lower.append(lax.ppermute(lower[-1] if lower else shard, axis, pairs))
+        else:
+            upper.append(lax.ppermute(upper[-1] if upper else shard, axis, back))
+    blocks = jnp.stack([*lower[::-1], shard, *upper])
+    shift = lax.axis_index(axis) - len(lower)
+    blocks = blocks[(jnp.arange(peers) - shift) % peers]
+    return laid_out(blocks, dim)
 
 
 def with_halo(cells, sides, width):
@@ -99,7 +121,7 @@
     first, keeps, pushes = cheb_table(CHEB)
     keep_table = jnp.asarray(np.array(keeps, np.float32))
     push_table = jnp.asarray(np.array(pushes, np.float32))
-    columns = lax.all_gather(panel, "test", axis=0, tiled=True)
+    columns = collect(panel, "test", 0)
     columns_all = columns.shape[0]
     perm = jnp.exp(log_perm)
     stacked = jnp.concatenate([perm[None], perm[None] * columns], axis=0)

time: 410 us -> 404 us (0.985)
  waiting for transfers between devices: 144 us -> 127 us
  starting transfers between devices: 97.2 us -> 103 us
    all_gather x1 -> x0, waiting for transfers between devices: 48.2 us -> none  [shards(): columns = lax.all_gather(panel, 'test', axis=0, tiled=True)]
    ppermute x0 -> x3, waiting for transfers between devices: none -> 32.7 us  [the longest x2 24.6 us: collect(): lower.append(lax.ppermute(lower[-1] if lower else shard, axis, pairs))]
    ppermute x0 -> x3, starting transfers between devices: none -> 5.08 us  [the longest x2 3.05 us: collect(): lower.append(lax.ppermute(lower[-1] if lower else shard, axis, pairs))]
  transfers between devices with their start and end apart: 32 -> 34, of which waited for: 8 -> 11; matrix products, arithmetic and copies ran while one was open for 8% -> 8% of each run, Pallas kernels for 0% -> 0%
where the time goes in v1:
time: 404 us; the launch traced here: 402 us
  waiting for transfers between devices  127 us (31%)
  other arithmetic  112 us (28%)
  starting transfers between devices  103 us (25%)
  local copies, waits for them, and re-layouts  45.7 us (11%)
  between operations  13.8 us (3%)
    psum x1, waiting for transfers between devices, shards(): total = lax.psum(partial_value, 'test')  89.3 us
    ppermute x15, starting transfers between devices, with_halo(): lax.ppermute(tail, axis, [(i, (i + 1) % count) for i in range(ends)])  78.7 us
    add x12, other arithmetic, sweep(): direction = keep_table[turn] * direction + push_table[turn] * residual  72.7 us
    ppermute x2, waiting for transfers between devices, collect(): lower.append(lax.ppermute(lower[-1] if lower else shard, axis, pairs))  24.6 us
    ppermute x15, starting transfers between devices, with_halo(): lax.ppermute(head, axis, [((i + 1) % count, i) for i in range(ends)])  19.3 us
    while x12, local copies, waits for them, and re-layouts  16.5 us
    dynamic_slice x24, local copies, waits for them, and re-layouts, sweep(): direction = keep_table[turn] * direction + push_table[turn] * residual  15.2 us
    mul x3, other arithmetic, solve(): direction = right_side * first  10.7 us
  transfers between devices with their start and end apart: 34, of which 11 were waited for; matrix products, arithmetic and copies ran while one was open for 8% of the time, Pallas kernels for 0%

profile of v1, /device:TPU:0, one launch (start us, length us, event | category | flops | bytes accessed | tf_op | source)
XLA Modules:
  0.0 401.6 jit_solution(11002438189142626333)
XLA Ops:
  11.6 13.0 %collective-permute-done.6 = f32[2,16,16,256]{3,2,1,0:T(8,128)S(1)} collective-permute-done((f32[2,16,16,256]{3,2,1,0:T(8,128)}, f32[2,16,16,256]{3,2,1,0:T(8,128)S(1)}, u32[]{:S(2)}, u32[]{:S(2)}) %collective-permute-start.6) | collective-permute-done | bytes 524320 | tf_op jit(solution)/shard_map/ppermute | solution.py:25
  26.6 8.1 %collective-permute-done.8 = f32[2,16,16,256]{3,2,1,0:T(8,128)S(1)} collective-permute-done((f32[2,16,16,256]{3,2,1,0:T(8,128)}, f32[2,16,16,256]{3,2,1,0:T(8,128)S(1)}, u32[]{:S(2)}, u32[]{:S(2)}) %collective-permute-start.8) | collective-permute-done | bytes 524320 | tf_op jit(solution)/shard_map/ppermute | solution.py:27
  34.7 11.6 %collective-permute-done.7 = f32[2,16,16,256]{3,2,1,0:T(8,128)S(1)} collective-permute-done((f32[2,16,16,256]{3,2,1,0:T(8,128)S(1)}, f32[2,16,16,256]{3,2,1,0:T(8,128)S(1)}, u32[]{:S(2)}, u32[]{:S(2)}) %collective-permute-start.7) | collective-permute-done | bytes 524320 | tf_op jit(solution)/shard_map/ppermute | solution.py:25
  63.0 51.5 %while.63 = (s32[]{:T(128)}, f32[1,16,16,256]{3,2,1,0:T(8,128)}, f32[1,16,16,256]{3,2,1,0:T(8,128)}, f32[1,16,16,256]{3,2,1,0:T(8,128)}, f32[16,16,256]{2,1,0:T(...) while((s32[]{:T(128)}, f32[1,16,16,256]{3,2,1,0:T(8,128)}, ...), condition=%wide.region_2.3_spmd.clone.clone, body=%wide.region_1.2_spmd.sunk.clone.clone.sunk | while | flops 2424835 | bytes 3637479 | solution.py:155
  64.0 7.4 %collective-permute-start = (f32[1,1,16,256]{3,2,1,0:T(8,128)S(1)}, f32[1,1,16,256]{3,2,1,0:T(8,128)S(1)}, u32[]{:S(2)}, u32[]{:S(2)}) collective-permute-start(f32[1,1,16,256]{3,2,1,0:T(8,128)S(1)} %get-tuple-element.979), channel_id=1, source_target_pairs={{0,1},{1,2},{2,3},{3,4},{4,5},{5,6},{6,7},{8,9},{9,10},{10,11},{11... | collective-permute-start | bytes 49160 | tf_op jit(solution)/shard_map/while/body/eval_jaxpr/ppermute | solution.py:42
  78.9 4.2 %collective-permute-start = (f32[1,1,16,256]{3,2,1,0:T(8,128)S(1)}, f32[1,1,16,256]{3,2,1,0:T(8,128)S(1)}, u32[]{:S(2)}, u32[]{:S(2)}) collective-permute-start(f32[1,1,16,256]{3,2,1,0:T(8,128)S(1)} %get-tuple-element.979), channel_id=1, source_target_pairs={{0,1},{1,2},{2,3},{3,4},{4,5},{5,6},{6,7},{8,9},{9,10},{10,11},{11... | collective-permute-start | bytes 49160 | tf_op jit(solution)/shard_map/while/body/eval_jaxpr/ppermute | solution.py:42
  86.2 3.5 multiply_add_fusion.6
  90.7 4.8 %collective-permute-start = (f32[1,1,16,256]{3,2,1,0:T(8,128)S(1)}, f32[1,1,16,256]{3,2,1,0:T(8,128)S(1)}, u32[]{:S(2)}, u32[]{:S(2)}) collective-permute-start(f32[1,1,16,256]{3,2,1,0:T(8,128)S(1)} %get-tuple-element.979), channel_id=1, source_target_pairs={{0,1},{1,2},{2,3},{3,4},{4,5},{5,6},{6,7},{8,9},{9,10},{10,11},{11... | collective-permute-start | bytes 49160 | tf_op jit(solution)/shard_map/while/body/eval_jaxpr/ppermute | solution.py:42
  103.1 4.8 %collective-permute-start = (f32[1,1,16,256]{3,2,1,0:T(8,128)S(1)}, f32[1,1,16,256]{3,2,1,0:T(8,128)S(1)}, u32[]{:S(2)}, u32[]{:S(2)}) collective-permute-start(f32[1,1,16,256]{3,2,1,0:T(8,128)S(1)} %get-tuple-element.979), channel_id=1, source_target_pairs={{0,1},{1,2},{2,3},{3,4},{4,5},{5,6},{6,7},{8,9},{9,10},{10,11},{11... | collective-permute-start | bytes 49160 | tf_op jit(solution)/shard_map/while/body/eval_jaxpr/ppermute | solution.py:42
  115.6 4.8 %collective-permute-start.11 = (f32[1,1,16,256]{3,2,1,0:T(8,128)S(1)}, f32[1,1,16,256]{3,2,1,0:T(8,128)S(1)}, u32[]{:S(2)}, u32[]{:S(2)}) collective-permute-start(f32[1,1,16,256]{3,2,1,0:T(8,128)S(1)} %get-tuple-element.831), channel_id=1, source_target_pairs={{0,1},{1,2},{2,3},{3,4},{4,5},{5,6},{6,7},{8,9},{9,10},{10,11},{11... | collective-permute-start | bytes 49160 | tf_op jit(solution)/shard_map/ppermute | solution.py:42
  125.9 4.0 broadcast_multiply_fusion.5
  129.9 76.5 %while.64 = (s32[]{:T(128)}, f32[8,16,16,256]{3,2,1,0:T(8,128)}, f32[8,16,16,256]{3,2,1,0:T(8,128)}, f32[8,16,16,256]{3,2,1,0:T(8,128)}, f32[16,16,256]{2,1,0:T(...) while((s32[]{:T(128)}, f32[8,16,16,256]{3,2,1,0:T(8,128)}, ...), condition=%wide.region_4.5_spmd.clone.clone, body=%wide.region_3.4_spmd.sunk.clone.clone.sunk | while | flops 14811139 | bytes 23068904 | solution.py:155
  132.2 4.5 %collective-permute-start.2 = (f32[8,1,16,256]{3,2,1,0:T(8,128)}, f32[8,1,16,256]{3,2,1,0:T(8,128)}, u32[]{:S(2)}, u32[]{:S(2)}) collective-permute-start(f32[8,1,16,256]{3,2,1,0:T(8,128)} %get-tuple-element.995), channel_id=1, source_target_pairs={{0,1},{1,2},{2,3},{3,4},{4,5},{5,6},{6,7},{8,9},{9,10},{10,11},{11... | collective-permute-start | bytes 393224 | tf_op jit(solution)/shard_map/while/body/eval_jaxpr/ppermute | solution.py:42
  140.5 7.1 %multiply_add_fusion.7 = (f32[8,16,16,256]{3,2,1,0:T(8,128)}, f32[8,16,16,256]{3,2,1,0:T(8,128)}, f32[8,16,16,256]{3,2,1,0:T(8,128)}) fusion(f32[8,16,16,256]{3,2,1,0:T(8,128)S(1)} %copy.50, f32[]{:T(128)} %bitcast.106, f32[]{:T(128)} %bitcast.107, f32[8,16,16,256]{3,2,1,0:T(8,128)} %get-tuple-element.1066, ...), kind=kLoop, calls=%fused_computation.70.clone.1 | loop fusion | flops 14155776 | bytes 14417929 | tf_op jit(solution)/shard_map/while/body/eval_jaxpr/add | solution.py:152
  149.9 6.1 %collective-permute-start.2 = (f32[8,1,16,256]{3,2,1,0:T(8,128)}, f32[8,1,16,256]{3,2,1,0:T(8,128)}, u32[]{:S(2)}, u32[]{:S(2)}) collective-permute-start(f32[8,1,16,256]{3,2,1,0:T(8,128)} %get-tuple-element.995), channel_id=1, source_target_pairs={{0,1},{1,2},{2,3},{3,4},{4,5},{5,6},{6,7},{8,9},{9,10},{10,11},{11... | collective-permute-start | bytes 393224 | tf_op jit(solution)/shard_map/while/body/eval_jaxpr/ppermute | solution.py:42
  159.6 7.5 %multiply_add_fusion.7 = (f32[8,16,16,256]{3,2,1,0:T(8,128)}, f32[8,16,16,256]{3,2,1,0:T(8,128)}, f32[8,16,16,256]{3,2,1,0:T(8,128)}) fusion(f32[8,16,16,256]{3,2,1,0:T(8,128)S(1)} %copy.50, f32[]{:T(128)} %bitcast.106, f32[]{:T(128)} %bitcast.107, f32[8,16,16,256]{3,2,1,0:T(8,128)} %get-tuple-element.1066, ...), kind=kLoop, calls=%fused_computation.70.clone.1 | loop fusion | flops 14155776 | bytes 14417929 | tf_op jit(solution)/shard_map/while/body/eval_jaxpr/add | solution.py:152
  169.4 6.7 %collective-permute-start.2 = (f32[8,1,16,256]{3,2,1,0:T(8,128)}, f32[8,1,16,256]{3,2,1,0:T(8,128)}, u32[]{:S(2)}, u32[]{:S(2)}) collective-permute-start(f32[8,1,16,256]{3,2,1,0:T(8,128)} %get-tuple-element.995), channel_id=1, source_target_pairs={{0,1},{1,2},{2,3},{3,4},{4,5},{5,6},{6,7},{8,9},{9,10},{10,11},{11... | collective-permute-start | bytes 393224 | tf_op jit(solution)/shard_map/while/body/eval_jaxpr/ppermute | solution.py:42
  179.7 7.5 %multiply_add_fusion.7 = (f32[8,16,16,256]{3,2,1,0:T(8,128)}, f32[8,16,16,256]{3,2,1,0:T(8,128)}, f32[8,16,16,256]{3,2,1,0:T(8,128)}) fusion(f32[8,16,16,256]{3,2,1,0:T(8,128)S(1)} %copy.50, f32[]{:T(128)} %bitcast.106, f32[]{:T(128)} %bitcast.107, f32[8,16,16,256]{3,2,1,0:T(8,128)} %get-tuple-element.1066, ...), kind=kLoop, calls=%fused_computation.70.clone.1 | loop fusion | flops 14155776 | bytes 14417929 | tf_op jit(solution)/shard_map/while/body/eval_jaxpr/add | solution.py:152
  189.5 5.8 %collective-permute-start.2 = (f32[8,1,16,256]{3,2,1,0:T(8,128)}, f32[8,1,16,256]{3,2,1,0:T(8,128)}, u32[]{:S(2)}, u32[]{:S(2)}) collective-permute-start(f32[8,1,16,256]{3,2,1,0:T(8,128)} %get-tuple-element.995), channel_id=1, source_target_pairs={{0,1},{1,2},{2,3},{3,4},{4,5},{5,6},{6,7},{8,9},{9,10},{10,11},{11... | collective-permute-start | bytes 393224 | tf_op jit(solution)/shard_map/while/body/eval_jaxpr/ppermute | solution.py:42
  198.9 7.5 %multiply_add_fusion.7 = (f32[8,16,16,256]{3,2,1,0:T(8,128)}, f32[8,16,16,256]{3,2,1,0:T(8,128)}, f32[8,16,16,256]{3,2,1,0:T(8,128)}) fusion(f32[8,16,16,256]{3,2,1,0:T(8,128)S(1)} %copy.50, f32[]{:T(128)} %bitcast.106, f32[]{:T(128)} %bitcast.107, f32[8,16,16,256]{3,2,1,0:T(8,128)} %get-tuple-element.1066, ...), kind=kLoop, calls=%fused_computation.70.clone.1 | loop fusion | flops 14155776 | bytes 14417929 | tf_op jit(solution)/shard_map/while/body/eval_jaxpr/add | solution.py:152
  206.4 5.0 %broadcast_multiply_fusion.4 = (f32[8,16,16,256]{3,2,1,0:T(8,128)}, f32[8,16,16,256]{3,2,1,0:T(8,128)}) fusion(f32[16,16,256]{2,1,0:T(8,128)} %add.657, f32[8,16,16,256]{3,2,1,0:T(8,128)} %get-tuple-element.571, f32[8,16,16,256]{3,2,1,0:T(8,128)} %get-tuple-element.572), kind=kLoop, calls=%fused_computation.183 | loop fusion | flops 1572864 | bytes 8650752 | tf_op jit(solution)/shard_map/mul | solution.py:144
  211.4 76.0 %while.65 = (s32[]{:T(128)}, f32[8,16,16,256]{3,2,1,0:T(8,128)}, f32[8,16,16,256]{3,2,1,0:T(8,128)}, f32[8,16,16,256]{3,2,1,0:T(8,128)}, f32[16,16,256]{2,1,0:T(...) while((s32[]{:T(128)}, f32[8,16,16,256]{3,2,1,0:T(8,128)}, ...), condition=%wide.region_7.8_spmd.clone.clone, body=%wide.region_6.7_spmd.sunk.clone.clone.sunk | while | flops 14811139 | bytes 23068904 | solution.py:155
  213.7 5.8 %collective-permute-start.4 = (f32[8,1,16,256]{3,2,1,0:T(8,128)}, f32[8,1,16,256]{3,2,1,0:T(8,128)}, u32[]{:S(2)}, u32[]{:S(2)}) collective-permute-start(f32[8,1,16,256]{3,2,1,0:T(8,128)} %get-tuple-element.1013), channel_id=1, source_target_pairs={{0,1},{1,2},{2,3},{3,4},{4,5},{5,6},{6,7},{8,9},{9,10},{10,11},{11... | collective-permute-start | bytes 393224 | tf_op jit(solution)/shard_map/while/body/eval_jaxpr/ppermute | solution.py:42
  223.1 7.0 %multiply_add_fusion.8 = (f32[8,16,16,256]{3,2,1,0:T(8,128)}, f32[8,16,16,256]{3,2,1,0:T(8,128)}, f32[8,16,16,256]{3,2,1,0:T(8,128)}) fusion(f32[8,16,16,256]{3,2,1,0:T(8,128)S(1)} %copy.51, f32[]{:T(128)} %bitcast.108, f32[]{:T(128)} %bitcast.109, f32[8,16,16,256]{3,2,1,0:T(8,128)} %get-tuple-element.1099, ...), kind=kLoop, calls=%fused_computation.111.clone.1 | loop fusion | flops 14155776 | bytes 14417929 | tf_op jit(solution)/shard_map/while/body/eval_jaxpr/add | solution.py:152
  232.4 5.8 %collective-permute-start.4 = (f32[8,1,16,256]{3,2,1,0:T(8,128)}, f32[8,1,16,256]{3,2,1,0:T(8,128)}, u32[]{:S(2)}, u32[]{:S(2)}) collective-permute-start(f32[8,1,16,256]{3,2,1,0:T(8,128)} %get-tuple-element.1013), channel_id=1, source_target_pairs={{0,1},{1,2},{2,3},{3,4},{4,5},{5,6},{6,7},{8,9},{9,10},{10,11},{11... | collective-permute-start | bytes 393224 | tf_op jit(solution)/shard_map/while/body/eval_jaxpr/ppermute | solution.py:42
  241.8 7.4 %multiply_add_fusion.8 = (f32[8,16,16,256]{3,2,1,0:T(8,128)}, f32[8,16,16,256]{3,2,1,0:T(8,128)}, f32[8,16,16,256]{3,2,1,0:T(8,128)}) fusion(f32[8,16,16,256]{3,2,1,0:T(8,128)S(1)} %copy.51, f32[]{:T(128)} %bitcast.108, f32[]{:T(128)} %bitcast.109, f32[8,16,16,256]{3,2,1,0:T(8,128)} %get-tuple-element.1099, ...), kind=kLoop, calls=%fused_computation.111.clone.1 | loop fusion | flops 14155776 | bytes 14417929 | tf_op jit(solution)/shard_map/while/body/eval_jaxpr/add | solution.py:152
  251.5 5.8 %collective-permute-start.4 = (f32[8,1,16,256]{3,2,1,0:T(8,128)}, f32[8,1,16,256]{3,2,1,0:T(8,128)}, u32[]{:S(2)}, u32[]{:S(2)}) collective-permute-start(f32[8,1,16,256]{3,2,1,0:T(8,128)} %get-tuple-element.1013), channel_id=1, source_target_pairs={{0,1},{1,2},{2,3},{3,4},{4,5},{5,6},{6,7},{8,9},{9,10},{10,11},{11... | collective-permute-start | bytes 393224 | tf_op jit(solution)/shard_map/while/body/eval_jaxpr/ppermute | solution.py:42
  260.9 7.4 %multiply_add_fusion.8 = (f32[8,16,16,256]{3,2,1,0:T(8,128)}, f32[8,16,16,256]{3,2,1,0:T(8,128)}, f32[8,16,16,256]{3,2,1,0:T(8,128)}) fusion(f32[8,16,16,256]{3,2,1,0:T(8,128)S(1)} %copy.51, f32[]{:T(128)} %bitcast.108, f32[]{:T(128)} %bitcast.109, f32[8,16,16,256]{3,2,1,0:T(8,128)} %get-tuple-element.1099, ...), kind=kLoop, calls=%fused_computation.111.clone.1 | loop fusion | flops 14155776 | bytes 14417929 | tf_op jit(solution)/shard_map/while/body/eval_jaxpr/add | solution.py:152
  270.6 5.8 %collective-permute-start.4 = (f32[8,1,16,256]{3,2,1,0:T(8,128)}, f32[8,1,16,256]{3,2,1,0:T(8,128)}, u32[]{:S(2)}, u32[]{:S(2)}) collective-permute-start(f32[8,1,16,256]{3,2,1,0:T(8,128)} %get-tuple-element.1013), channel_id=1, source_target_pairs={{0,1},{1,2},{2,3},{3,4},{4,5},{5,6},{6,7},{8,9},{9,10},{10,11},{11... | collective-permute-start | bytes 393224 | tf_op jit(solution)/shard_map/while/body/eval_jaxpr/ppermute | solution.py:42
  280.0 7.4 %multiply_add_fusion.8 = (f32[8,16,16,256]{3,2,1,0:T(8,128)}, f32[8,16,16,256]{3,2,1,0:T(8,128)}, f32[8,16,16,256]{3,2,1,0:T(8,128)}) fusion(f32[8,16,16,256]{3,2,1,0:T(8,128)S(1)} %copy.51, f32[]{:T(128)} %bitcast.108, f32[]{:T(128)} %bitcast.109, f32[8,16,16,256]{3,2,1,0:T(8,128)} %get-tuple-element.1099, ...), kind=kLoop, calls=%fused_computation.111.clone.1 | loop fusion | flops 14155776 | bytes 14417929 | tf_op jit(solution)/shard_map/while/body/eval_jaxpr/add | solution.py:152
  290.1 5.2 %collective-permute-start.13 = (f32[8,1,16,256]{3,2,1,0:T(8,128)S(1)}, f32[8,1,16,256]{3,2,1,0:T(8,128)S(1)}, u32[]{:S(2)}, u32[]{:S(2)}) collective-permute-start(f32[8,1,16,256]{3,2,1,0:T(8,128)S(1)} %get-tuple-element.818), channel_id=1, source_target_pairs={{0,1},{1,2},{2,3},{3,4},{4,5},{5,6},{6,7},{8,9},{9,10},{10,11},{11... | collective-permute-start | bytes 393224 | tf_op jit(solution)/shard_map/ppermute | solution.py:42
  303.6 89.3 %all-reduce.20.cloned.1.call-done = f32[8,16,16,256]{3,2,1,0:T(8,128)} async-done(((f32[8,16,16,256]{3,2,1,0:T(8,128)}), f32[8,16,16,256]{3,2,1,0:T(8,128)}) %all-reduce.20.cloned.1.call-update) | async-done | bytes 2097168 | tf_op jit(solution)/shard_map/psum | solution.py:172
  (199 shorter events, 116.9 us)
Async XLA Ops:
  6.5 386.4 %all-reduce.20.cloned.1.call-start = ((), (), s32[]{:S(2)}) async-start(), calls=%async_computation | async-start | bytes 4194304 | tf_op jit(solution)/shard_map/psum | solution.py:172
  6.5 18.1 %collective-permute-start.6 = (f32[2,16,16,256]{3,2,1,0:T(8,128)}, f32[2,16,16,256]{3,2,1,0:T(8,128)S(1)}, u32[]{:S(2)}, u32[]{:S(2)}) collective-permute-start(f32[2,16,16,256]{3,2,1,0:T(8,128)} %param.15), channel_id=1, source_target_pairs={{0,8},{8,16},{16,24},{24,0},{1,9},{9,17},{17,25},{25,1},{2,10},{10... | collective-permute-start | bytes 1572872 | tf_op jit(solution)/shard_map/ppermute | solution.py:25
  9.6 25.1 %collective-permute-start.8 = (f32[2,16,16,256]{3,2,1,0:T(8,128)}, f32[2,16,16,256]{3,2,1,0:T(8,128)S(1)}, u32[]{:S(2)}, u32[]{:S(2)}) collective-permute-start(f32[2,16,16,256]{3,2,1,0:T(8,128)} %param.15), channel_id=1, source_target_pairs={{8,0},{16,8},{24,16},{0,24},{9,1},{17,9},{25,17},{1,25},{10,2},{18... | collective-permute-start | bytes 1572872 | tf_op jit(solution)/shard_map/ppermute | solution.py:27
  24.6 21.6 %collective-permute-start.7 = (f32[2,16,16,256]{3,2,1,0:T(8,128)S(1)}, f32[2,16,16,256]{3,2,1,0:T(8,128)S(1)}, u32[]{:S(2)}, u32[]{:S(2)}) collective-permute-start(f32[2,16,16,256]{3,2,1,0:T(8,128)S(1)} %collective-permute-done.6), channel_id=1, source_target_pairs={{0,8},{8,16},{16,24},{24,0},{1,9},{9,17},{17,25},{25,1},{2,10},{10... | collective-permute-start | bytes 1572872 | tf_op jit(solution)/shard_map/ppermute | solution.py:25
  53.7 6.2 %collective-permute-start.10 = (f32[9,2,16,256]{3,2,1,0:T(8,128)}, f32[9,2,16,256]{3,2,1,0:T(8,128)S(1)}, u32[]{:S(2)}, u32[]{:S(2)}) collective-permute-start(f32[9,2,16,256]{3,2,1,0:T(8,128)} %get-tuple-element.816), channel_id=1, source_target_pairs={{0,1},{1,2},{2,3},{3,4},{4,5},{5,6},{6,7},{8,9},{9,10},{10,11},{11... | collective-permute-start | bytes 884744 | tf_op jit(solution)/shard_map/ppermute | solution.py:42
  55.0 5.4 %collective-permute-start.9 = (f32[9,2,16,256]{3,2,1,0:T(8,128)}, f32[9,2,16,256]{3,2,1,0:T(8,128)S(1)}, u32[]{:S(2)}, u32[]{:S(2)}) collective-permute-start(f32[9,2,16,256]{3,2,1,0:T(8,128)} %get-tuple-element.817), channel_id=1, source_target_pairs={{1,0},{2,1},{3,2},{4,3},{5,4},{6,5},{7,6},{9,8},{10,9},{11,10},{12... | collective-permute-start | bytes 884744 | tf_op jit(solution)/shard_map/ppermute | solution.py:44
  64.0 9.9 %collective-permute-start = (f32[1,1,16,256]{3,2,1,0:T(8,128)S(1)}, f32[1,1,16,256]{3,2,1,0:T(8,128)S(1)}, u32[]{:S(2)}, u32[]{:S(2)}) collective-permute-start(f32[1,1,16,256]{3,2,1,0:T(8,128)S(1)} %get-tuple-element.979), channel_id=1, source_target_pairs={{0,1},{1,2},{2,3},{3,4},{4,5},{5,6},{6,7},{8,9},{9,10},{10,11},{11... | collective-permute-start | bytes 49160 | tf_op jit(solution)/shard_map/while/body/eval_jaxpr/ppermute | solution.py:42
  71.4 3.1 collective-permute-start.1
  78.9 6.8 %collective-permute-start = (f32[1,1,16,256]{3,2,1,0:T(8,128)S(1)}, f32[1,1,16,256]{3,2,1,0:T(8,128)S(1)}, u32[]{:S(2)}, u32[]{:S(2)}) collective-permute-start(f32[1,1,16,256]{3,2,1,0:T(8,128)S(1)} %get-tuple-element.979), channel_id=1, source_target_pairs={{0,1},{1,2},{2,3},{3,4},{4,5},{5,6},{6,7},{8,9},{9,10},{10,11},{11... | collective-permute-start | bytes 49160 | tf_op jit(solution)/shard_map/while/body/eval_jaxpr/ppermute | solution.py:42
  83.1 3.1 collective-permute-start.1
  90.7 7.3 %collective-permute-start = (f32[1,1,16,256]{3,2,1,0:T(8,128)S(1)}, f32[1,1,16,256]{3,2,1,0:T(8,128)S(1)}, u32[]{:S(2)}, u32[]{:S(2)}) collective-permute-start(f32[1,1,16,256]{3,2,1,0:T(8,128)S(1)} %get-tuple-element.979), channel_id=1, source_target_pairs={{0,1},{1,2},{2,3},{3,4},{4,5},{5,6},{6,7},{8,9},{9,10},{10,11},{11... | collective-permute-start | bytes 49160 | tf_op jit(solution)/shard_map/while/body/eval_jaxpr/ppermute | solution.py:42
  103.1 7.4 %collective-permute-start = (f32[1,1,16,256]{3,2,1,0:T(8,128)S(1)}, f32[1,1,16,256]{3,2,1,0:T(8,128)S(1)}, u32[]{:S(2)}, u32[]{:S(2)}) collective-permute-start(f32[1,1,16,256]{3,2,1,0:T(8,128)S(1)} %get-tuple-element.979), channel_id=1, source_target_pairs={{0,1},{1,2},{2,3},{3,4},{4,5},{5,6},{6,7},{8,9},{9,10},{10,11},{11... | collective-permute-start | bytes 49160 | tf_op jit(solution)/shard_map/while/body/eval_jaxpr/ppermute | solution.py:42
  115.6 8.9 %collective-permute-start.11 = (f32[1,1,16,256]{3,2,1,0:T(8,128)S(1)}, f32[1,1,16,256]{3,2,1,0:T(8,128)S(1)}, u32[]{:S(2)}, u32[]{:S(2)}) collective-permute-start(f32[1,1,16,256]{3,2,1,0:T(8,128)S(1)} %get-tuple-element.831), channel_id=1, source_target_pairs={{0,1},{1,2},{2,3},{3,4},{4,5},{5,6},{6,7},{8,9},{9,10},{10,11},{11... | collective-permute-start | bytes 49160 | tf_op jit(solution)/shard_map/ppermute | solution.py:42
  120.4 4.1 %collective-permute-start.12 = (f32[1,1,16,256]{3,2,1,0:T(8,128)S(1)}, f32[1,1,16,256]{3,2,1,0:T(8,128)S(1)}, u32[]{:S(2)}, u32[]{:S(2)}) collective-permute-start(f32[1,1,16,256]{3,2,1,0:T(8,128)S(1)} %get-tuple-element.832), channel_id=1, source_target_pairs={{1,0},{2,1},{3,2},{4,3},{5,4},{6,5},{7,6},{9,8},{10,9},{11,10},{12... | collective-permute-start | bytes 49160 | tf_op jit(solution)/shard_map/ppermute | solution.py:44
  132.2 8.1 %collective-permute-start.2 = (f32[8,1,16,256]{3,2,1,0:T(8,128)}, f32[8,1,16,256]{3,2,1,0:T(8,128)}, u32[]{:S(2)}, u32[]{:S(2)}) collective-permute-start(f32[8,1,16,256]{3,2,1,0:T(8,128)} %get-tuple-element.995), channel_id=1, source_target_pairs={{0,1},{1,2},{2,3},{3,4},{4,5},{5,6},{6,7},{8,9},{9,10},{10,11},{11... | collective-permute-start | bytes 393224 | tf_op jit(solution)/shard_map/while/body/eval_jaxpr/ppermute | solution.py:42
  136.6 3.8 collective-permute-start.3
  149.9 9.7 %collective-permute-start.2 = (f32[8,1,16,256]{3,2,1,0:T(8,128)}, f32[8,1,16,256]{3,2,1,0:T(8,128)}, u32[]{:S(2)}, u32[]{:S(2)}) collective-permute-start(f32[8,1,16,256]{3,2,1,0:T(8,128)} %get-tuple-element.995), channel_id=1, source_target_pairs={{0,1},{1,2},{2,3},{3,4},{4,5},{5,6},{6,7},{8,9},{9,10},{10,11},{11... | collective-permute-start | bytes 393224 | tf_op jit(solution)/shard_map/while/body/eval_jaxpr/ppermute | solution.py:42
  156.0 3.6 collective-permute-start.3
  169.4 10.3 %collective-permute-start.2 = (f32[8,1,16,256]{3,2,1,0:T(8,128)}, f32[8,1,16,256]{3,2,1,0:T(8,128)}, u32[]{:S(2)}, u32[]{:S(2)}) collective-permute-start(f32[8,1,16,256]{3,2,1,0:T(8,128)} %get-tuple-element.995), channel_id=1, source_target_pairs={{0,1},{1,2},{2,3},{3,4},{4,5},{5,6},{6,7},{8,9},{9,10},{10,11},{11... | collective-permute-start | bytes 393224 | tf_op jit(solution)/shard_map/while/body/eval_jaxpr/ppermute | solution.py:42
  176.1 3.6 collective-permute-start.3
  189.5 9.4 %collective-permute-start.2 = (f32[8,1,16,256]{3,2,1,0:T(8,128)}, f32[8,1,16,256]{3,2,1,0:T(8,128)}, u32[]{:S(2)}, u32[]{:S(2)}) collective-permute-start(f32[8,1,16,256]{3,2,1,0:T(8,128)} %get-tuple-element.995), channel_id=1, source_target_pairs={{0,1},{1,2},{2,3},{3,4},{4,5},{5,6},{6,7},{8,9},{9,10},{10,11},{11... | collective-permute-start | bytes 393224 | tf_op jit(solution)/shard_map/while/body/eval_jaxpr/ppermute | solution.py:42
  195.3 3.6 collective-permute-start.3
  213.7 9.4 %collective-permute-start.4 = (f32[8,1,16,256]{3,2,1,0:T(8,128)}, f32[8,1,16,256]{3,2,1,0:T(8,128)}, u32[]{:S(2)}, u32[]{:S(2)}) collective-permute-start(f32[8,1,16,256]{3,2,1,0:T(8,128)} %get-tuple-element.1013), channel_id=1, source_target_pairs={{0,1},{1,2},{2,3},{3,4},{4,5},{5,6},{6,7},{8,9},{9,10},{10,11},{11... | collective-permute-start | bytes 393224 | tf_op jit(solution)/shard_map/while/body/eval_jaxpr/ppermute | solution.py:42
  219.5 3.6 collective-permute-start.5
  232.4 9.4 %collective-permute-start.4 = (f32[8,1,16,256]{3,2,1,0:T(8,128)}, f32[8,1,16,256]{3,2,1,0:T(8,128)}, u32[]{:S(2)}, u32[]{:S(2)}) collective-permute-start(f32[8,1,16,256]{3,2,1,0:T(8,128)} %get-tuple-element.1013), channel_id=1, source_target_pairs={{0,1},{1,2},{2,3},{3,4},{4,5},{5,6},{6,7},{8,9},{9,10},{10,11},{11... | collective-permute-start | bytes 393224 | tf_op jit(solution)/shard_map/while/body/eval_jaxpr/ppermute | solution.py:42
  238.2 3.6 collective-permute-start.5
  251.5 9.4 %collective-permute-start.4 = (f32[8,1,16,256]{3,2,1,0:T(8,128)}, f32[8,1,16,256]{3,2,1,0:T(8,128)}, u32[]{:S(2)}, u32[]{:S(2)}) collective-permute-start(f32[8,1,16,256]{3,2,1,0:T(8,128)} %get-tuple-element.1013), channel_id=1, source_target_pairs={{0,1},{1,2},{2,3},{3,4},{4,5},{5,6},{6,7},{8,9},{9,10},{10,11},{11... | collective-permute-start | bytes 393224 | tf_op jit(solution)/shard_map/while/body/eval_jaxpr/ppermute | solution.py:42
  257.3 3.6 collective-permute-start.5
  270.6 9.4 %collective-permute-start.4 = (f32[8,1,16,256]{3,2,1,0:T(8,128)}, f32[8,1,16,256]{3,2,1,0:T(8,128)}, u32[]{:S(2)}, u32[]{:S(2)}) collective-permute-start(f32[8,1,16,256]{3,2,1,0:T(8,128)} %get-tuple-element.1013), channel_id=1, source_target_pairs={{0,1},{1,2},{2,3},{3,4},{4,5},{5,6},{6,7},{8,9},{9,10},{10,11},{11... | collective-permute-start | bytes 393224 | tf_op jit(solution)/shard_map/while/body/eval_jaxpr/ppermute | solution.py:42
  276.4 3.6 collective-permute-start.5
  290.1 6.5 %collective-permute-start.13 = (f32[8,1,16,256]{3,2,1,0:T(8,128)S(1)}, f32[8,1,16,256]{3,2,1,0:T(8,128)S(1)}, u32[]{:S(2)}, u32[]{:S(2)}) collective-permute-start(f32[8,1,16,256]{3,2,1,0:T(8,128)S(1)} %get-tuple-element.818), channel_id=1, source_target_pairs={{0,1},{1,2},{2,3},{3,4},{4,5},{5,6},{6,7},{8,9},{9,10},{10,11},{11... | collective-permute-start | bytes 393224 | tf_op jit(solution)/shard_map/ppermute | solution.py:42
  295.3 3.2 collective-permute-start.14
  (22 other events, 100.4 us)
Sparse Core Ops, SparseCore 0:
  303.7 89.1 all-reduce.19
